TPU v7x, 32 devices: a whole 2x2x4 slice. The times are simulated.
32 devices in a mesh: gx: 4 (over x, core), gy: 8 (over z, y).
Axes of the slice: x: 2, y: 2, z: 4, core: 2. Of those that a mesh axis runs over, the one named last changes fastest.
Arguments:
- right_side: float32 [4, 1024, 2048], P(None, 'gx', 'gy')
- prior_weight: float32 [4, 1024, 2048], P(None, 'gx', 'gy'), may hold values from 0.5 to 4
- jacobi_inverse: float32 [4, 1024, 2048], P(None, 'gx', 'gy'), may hold values from 0.1 to 0.5
- interaction: float32 [2, 4, 128, 128], replicated, may hold values from -0.5 to 0.5
- footprint: int32 [2, 16, 16, 4], P(None, 'gx', 'gy'), may hold values from 0 to 255, as said below
Outputs:
- solution: float32 [4, 1024, 2048], P(None, 'gx', 'gy')
- residual: float32 [4, 1024, 2048], P(None, 'gx', 'gy')
Inputs may be any that keep to these rules, and one draw needn't show every extreme that they name: `footprint`: each entry is bx * 16 + by of a block of the same 4 block rows along the first dimension as its ray block's tile. Of the 64 entries of one tile's ray blocks, between 7 and 9 fall in each tile of the same strip along the second dimension, exactly 9 in some; one tile of the second dimension receives exactly 9 entries from every tile of the strip.
All inputs are finite; a program needn't handle non-finite values.
Results may differ from a plain program's by a relative error of at most 0.0003.
Values sent between devices are 32-bit elements; how exact they have to be, the bound alone decides.
No kernel may reach another device: no remote copies, remote signals or barrier semaphores. Data moves between devices by JAX's collectives and lax.ppermute only.
A program may use at most 128 MiB of HBM per device.

v0:
```python
import jax
import jax.numpy as jnp
from jax import lax
from jax.sharding import PartitionSpec as P

ITERS = 4
DAUB_LOW = (
    0.3326705529509569,
    0.8068915093133388,
    0.4598775021193313,
    -0.13501102001039084,
    -0.08544127388224149,
    0.035226291882100656,
)
DAUB_HIGH = tuple(((-1.0) ** tap_index * DAUB_LOW[5 - tap_index] for tap_index in range(6)))


def extended(block, sides, width):
    for axis, dim in sides:
        count = lax.axis_size(axis)
        forward = [(i, i + 1) for i in range(count - 1)]
        backward = [(target, source) for source, target in forward]
        low = lax.ppermute(
            lax.slice_in_dim(block, block.shape[dim] - width, None, axis=dim), axis, forward
        )
        high = lax.ppermute(lax.slice_in_dim(block, 0, width, axis=dim), axis, backward)
        block = jnp.concatenate([low, block, high], axis=dim)
    return block


def synth_table(length):
    inputs = jnp.arange(length + 8, dtype=jnp.int32)[:, None]
    outputs = jnp.arange(length, dtype=jnp.int32)[None, :]
    half = outputs // 2
    phase = outputs % 2
    table = jnp.zeros((length + 8, length), jnp.float32)
    for tap_num in range(3):
        low_coef = jnp.where(phase == 0, DAUB_LOW[2 * tap_num], DAUB_LOW[2 * tap_num + 1])
        high_coef = jnp.where(phase == 0, DAUB_HIGH[2 * tap_num], DAUB_HIGH[2 * tap_num + 1])
        table = table + jnp.where(inputs == 2 * (half - tap_num) + 4, low_coef, 0.0)
        table = table + jnp.where(inputs == 2 * (half - tap_num) + 5, high_coef, 0.0)
    return table


def analysis_table(length):
    inputs = jnp.arange(length + 8, dtype=jnp.int32)[:, None]
    outputs = jnp.arange(length, dtype=jnp.int32)[None, :]
    half = outputs // 2
    phase = outputs % 2
    table = jnp.zeros((length + 8, length), jnp.float32)
    for tap_num in range(3):
        for offset in (0, 1):
            coef = jnp.where(
                phase == 0, DAUB_LOW[2 * tap_num + offset], DAUB_HIGH[2 * tap_num + offset]
            )
            table = table + jnp.where(inputs == 2 * (half + tap_num) + offset + 4, coef, 0.0)
    return table


def with_rim(field):
    return extended(field, (("gx", 1), ("gy", 2)), 4)


def shards(right_side, prior_weight, jacobi_inverse, interaction, footprint):
    highest = lax.Precision.HIGHEST
    layers, tile_rows, tile_cols = right_side.shape
    sensors, rows_blocks, cols_blocks = (footprint.shape[0], footprint.shape[1], footprint.shape[2])
    block_rows = tile_rows // rows_blocks
    block_cols = tile_cols // cols_blocks
    owners = lax.axis_size("gy")
    layer_blocks_cols = cols_blocks * owners
    requests = sensors * rows_blocks * cols_blocks * layers
    capacity = requests // owners + 1
    own_blocks = layers * rows_blocks * cols_blocks
    synth_rows = synth_table(tile_rows)
    synth_cols = synth_table(tile_cols)
    analysis_rows = analysis_table(tile_rows)
    analysis_cols = analysis_table(tile_cols)
    flat_ids = footprint.reshape(requests)
    request_num = jnp.arange(requests, dtype=jnp.int32)
    layer_of = request_num % layers
    sensor_of = request_num // (requests // sensors)
    target = flat_ids % layer_blocks_cols // cols_blocks
    owned_index = (
        layer_of * (rows_blocks * cols_blocks)
        + flat_ids // layer_blocks_cols % rows_blocks * cols_blocks
        + flat_ids % layer_blocks_cols % cols_blocks
    )
    picks = (target[:, None] == jnp.arange(owners, dtype=jnp.int32)[None, :]).astype(jnp.int32)
    slot = jnp.sum(picks * (jnp.cumsum(picks, axis=0) - 1), axis=1)
    send_ids = jnp.full((owners, capacity), own_blocks, jnp.int32).at[target, slot].set(owned_index)
    send_pairs = (
        jnp.zeros((owners, capacity), jnp.int32).at[target, slot].set(sensor_of * layers + layer_of)
    )
    wanted_ids, wanted_pairs = (
        lax.all_to_all(send_ids, "gy", split_axis=0, concat_axis=0, tiled=True),
        lax.all_to_all(send_pairs, "gy", split_axis=0, concat_axis=0, tiled=True),
    )
    slot_source = (
        jnp.full((owners, capacity), requests, jnp.int32).at[target, slot].set(request_num)
    )
    landing = (
        wanted_ids.reshape(-1)[None, :] == jnp.arange(own_blocks, dtype=jnp.int32)[:, None]
    ).astype(jnp.float32)
    solution = jnp.zeros_like(right_side)
    residual = right_side
    precond_res = jacobi_inverse * residual

    def global_sum(local_value):
        return lax.psum(local_value, ("gx", "gy"))

    direction = precond_res
    rho_now = global_sum(jnp.sum(residual * precond_res))
    for step in range(ITERS):
        synthesize_padded = with_rim(direction)
        along_rows = jnp.einsum("lab,ac->lcb", synthesize_padded, synth_rows, precision=highest)
        blocks = (
            jnp.einsum("lab,bc->lac", along_rows, synth_cols, precision=highest)
            .reshape(layers, rows_blocks, block_rows, cols_blocks, block_cols)
            .transpose(0, 1, 3, 2, 4)
            .reshape(own_blocks, block_rows, block_cols)
        )
        outgoing = jnp.take(blocks, wanted_ids, axis=0, mode="fill", fill_value=0.0)
        arrived = lax.all_to_all(outgoing, "gy", split_axis=0, concat_axis=0, tiled=True)
        seen = arrived[target, slot].reshape(
            sensors, rows_blocks * cols_blocks, layers, block_rows, block_cols
        )
        slopes = jnp.einsum("sklxy,slyz->skxz", seen, interaction, precision=highest)
        back = jnp.einsum("skxz,slyz->sklxy", slopes, interaction, precision=highest).reshape(
            requests, block_rows, block_cols
        )
        returning = jnp.take(back, slot_source, axis=0, mode="fill", fill_value=0.0)
        landed = lax.all_to_all(returning, "gy", split_axis=0, concat_axis=0, tiled=True)
        summed = jnp.dot(
            landing, landed.reshape(owners * capacity, block_rows * block_cols), precision=highest
        )
        padded = with_rim(
            summed.reshape(layers, rows_blocks, cols_blocks, block_rows, block_cols)
            .transpose(0, 1, 3, 2, 4)
            .reshape(layers, tile_rows, tile_cols)
        )
        along_cols = jnp.einsum("lab,bc->lac", padded, analysis_cols, precision=highest)
        image = (
            jnp.einsum("lab,ac->lcb", along_cols, analysis_rows, precision=highest)
            + prior_weight * direction
        )
        step_size = rho_now / global_sum(jnp.sum(direction * image))
        solution = solution + step_size * direction
        residual = residual - step_size * image
        if step + 1 < ITERS:
            precond_res = jacobi_inverse * residual
            rho_next = global_sum(jnp.sum(residual * precond_res))
            direction = precond_res + rho_next / rho_now * direction
            rho_now = rho_next
    return (solution, residual)


def solution(mesh):
    return jax.shard_map(
        shards,
        mesh=mesh,
        in_specs=(
            P(None, "gx", "gy"),
            P(None, "gx", "gy"),
            P(None, "gx", "gy"),
            P(),
            P(None, "gx", "gy", None),
        ),
        out_specs=(P(None, "gx", "gy"), P(None, "gx", "gy")),
        check_vma=False,
    )
```

profile of v0, /device:TPU:0, one launch (start us, length us, event | category | flops | bytes accessed | tf_op | source)
XLA Modules:
  0.0 1154.9 jit_solution(17234243243100346092)
XLA Ops:
  3.4 10.1 scatter_fusion
  13.5 7.3 all-to-all-start
  33.4 3.9 collective-permute-start.2
  38.8 4.2 collective-permute-done.3
  56.5 5.7 all-to-all-start.1
  65.8 48.2 %all-to-all-done.1 = f32[8,9,64,128]{3,2,1,0:T(8,128)} async-done(((f32[8,9,64,128]{3,2,1,0:T(8,128)}), f32[8,9,64,128]{3,2,1,0:T(8,128)}, u32[]{:S(2)}, u32[]{:S(2)}) %all-to-all-start.1) | async-done | bytes 2359328 | tf_op jit(solution)/shard_map/all_to_all | solution.py:124
  124.3 3.7 gather_fusion.5
  131.4 7.1 all-to-all-start.2
  139.8 54.4 %all-to-all-done.2 = f32[8,9,64,128]{3,2,1,0:T(8,128)} async-done(((f32[8,9,64,128]{3,2,1,0:T(8,128)}), f32[8,9,64,128]{3,2,1,0:T(8,128)}, u32[]{:S(2)}, u32[]{:S(2)}) %all-to-all-start.2) | async-done | bytes 2359328 | tf_op jit(solution)/shard_map/all_to_all | solution.py:133
  213.3 4.5 collective-permute-start.6
  220.8 3.8 fusion.18
  224.6 4.6 multiply_reduce_fusion.6
  229.2 41.6 %all-reduce = (f32[]{:T(128)}, f32[]{:T(128)}) all-reduce(f32[]{:T(128)} %get-tuple-element.7, f32[]{:T(128)} %get-tuple-element.6), channel_id=1, replica_groups=mesh['gx'=4,'gy'=8] {'gx','gy'}, use_global_device_ids=true, to_apply=%region_1.2 | all-reduce | flops 2 | bytes 16 | tf_op jit(solution)/shard_map/psum | solution.py:110
  272.0 4.0 multiply_reduce_fusion.5
  276.0 40.2 %psum.58 = f32[]{:T(128)} all-reduce(f32[]{:T(128)} %get-tuple-element.16), channel_id=1, replica_groups=mesh['gx'=4,'gy'=8] {'gx','gy'}, use_global_device_ids=true, to_apply=%region_9.12 | all-reduce | flops 1 | bytes 8 | tf_op jit(solution)/shard_map/psum | solution.py:110
  321.8 4.8 collective-permute-done.9
  331.4 4.6 collective-permute-done.11
  338.3 3.8 fusion.199
  352.4 57.1 %all_to_all.52 = f32[8,9,64,128]{3,2,1,0:T(8,128)} all-to-all(f32[8,9,64,128]{3,2,1,0:T(8,128)S(1)} %broadcast_select_fusion.5), channel_id=1, replica_groups=mesh['gx'=4,'gy'=8] {'gy'}, dimensions={0} | all-to-all | bytes 4718592 | tf_op jit(solution)/shard_map/all_to_all | solution.py:124
  409.5 3.7 gather_fusion.1
  425.5 59.7 %all_to_all.53 = f32[8,9,64,128]{3,2,1,0:T(8,128)S(1)} all-to-all(f32[8,9,64,128]{3,2,1,0:T(8,128)S(1)} %broadcast_select_fusion.4), channel_id=1, replica_groups=mesh['gx'=4,'gy'=8] {'gy'}, dimensions={0} | all-to-all | bytes 4718592 | tf_op jit(solution)/shard_map/all_to_all | solution.py:133
  509.4 4.0 collective-permute-done.15
  514.4 3.8 fusion.38
  518.2 4.5 multiply_reduce_fusion.4
  522.7 40.1 %psum.59 = f32[]{:T(128)} all-reduce(f32[]{:T(128)} %get-tuple-element.57), channel_id=1, replica_groups=mesh['gx'=4,'gy'=8] {'gx','gy'}, use_global_device_ids=true, to_apply=%region_11.14 | all-reduce | flops 1 | bytes 8 | tf_op jit(solution)/shard_map/psum | solution.py:110
  564.2 4.1 multiply_reduce_fusion.3
  568.3 40.2 %psum.60 = f32[]{:T(128)} all-reduce(f32[]{:T(128)} %get-tuple-element.13), channel_id=1, replica_groups=mesh['gx'=4,'gy'=8] {'gx','gy'}, use_global_device_ids=true, to_apply=%region_13.16 | all-reduce | flops 1 | bytes 8 | tf_op jit(solution)/shard_map/psum | solution.py:110
  614.2 4.8 collective-permute-done.17
  619.1 3.7 collective-permute-start.18
  624.4 4.2 collective-permute-done.19
  631.0 3.8 fusion.196
  645.0 56.2 %all_to_all.54 = f32[8,9,64,128]{3,2,1,0:T(8,128)} all-to-all(f32[8,9,64,128]{3,2,1,0:T(8,128)S(1)} %broadcast_select_fusion.3), channel_id=1, replica_groups=mesh['gx'=4,'gy'=8] {'gy'}, dimensions={0} | all-to-all | bytes 4718592 | tf_op jit(solution)/shard_map/all_to_all | solution.py:124
  717.1 60.0 %all_to_all.55 = f32[8,9,64,128]{3,2,1,0:T(8,128)S(1)} all-to-all(f32[8,9,64,128]{3,2,1,0:T(8,128)S(1)} %broadcast_select_fusion.2), channel_id=1, replica_groups=mesh['gx'=4,'gy'=8] {'gy'}, dimensions={0} | all-to-all | bytes 4718592 | tf_op jit(solution)/shard_map/all_to_all | solution.py:133
  801.3 4.0 collective-permute-done.23
  806.4 3.9 fusion.58
  810.3 4.5 multiply_reduce_fusion.2
  814.8 40.2 %psum.61 = f32[]{:T(128)} all-reduce(f32[]{:T(128)} %get-tuple-element.59), channel_id=1, replica_groups=mesh['gx'=4,'gy'=8] {'gx','gy'}, use_global_device_ids=true, to_apply=%region_15.18 | all-reduce | flops 1 | bytes 8 | tf_op jit(solution)/shard_map/psum | solution.py:110
  856.3 4.1 multiply_reduce_fusion.1
  860.4 40.1 %psum.62 = f32[]{:T(128)} all-reduce(f32[]{:T(128)} %get-tuple-element.10), channel_id=1, replica_groups=mesh['gx'=4,'gy'=8] {'gx','gy'}, use_global_device_ids=true, to_apply=%region_17.20 | all-reduce | flops 1 | bytes 8 | tf_op jit(solution)/shard_map/psum | solution.py:110
  906.5 4.8 collective-permute-done.25
  916.6 4.2 collective-permute-done.27
  923.2 3.8 fusion.193
  937.3 56.3 %all_to_all.56 = f32[8,9,64,128]{3,2,1,0:T(8,128)} all-to-all(f32[8,9,64,128]{3,2,1,0:T(8,128)S(1)} %broadcast_select_fusion.1), channel_id=1, replica_groups=mesh['gx'=4,'gy'=8] {'gy'}, dimensions={0} | all-to-all | bytes 4718592 | tf_op jit(solution)/shard_map/all_to_all | solution.py:124
  1009.5 59.9 %all_to_all.57 = f32[8,9,64,128]{3,2,1,0:T(8,128)S(1)} all-to-all(f32[8,9,64,128]{3,2,1,0:T(8,128)S(1)} %broadcast_select_fusion), channel_id=1, replica_groups=mesh['gx'=4,'gy'=8] {'gy'}, dimensions={0} | all-to-all | bytes 4718592 | tf_op jit(solution)/shard_map/all_to_all | solution.py:133
  1093.7 3.9 collective-permute-done.31
  1098.7 3.9 fusion.78
  1102.6 4.5 multiply_reduce_fusion
  1107.1 40.2 %psum.63 = f32[]{:T(128)} all-reduce(f32[]{:T(128)} %get-tuple-element.61), channel_id=1, replica_groups=mesh['gx'=4,'gy'=8] {'gx','gy'}, use_global_device_ids=true, to_apply=%region_19.22 | all-reduce | flops 1 | bytes 8 | tf_op jit(solution)/shard_map/psum | solution.py:110
  (225 shorter events, 259.1 us)
Async XLA Ops:
  0.6 117.1 %copy-start = (f32[2,4,128,128]{3,2,1,0:T(8,128)S(1)}, f32[2,4,128,128]{3,2,1,0:T(8,128)}, u32[]{:S(2)}) copy-start(f32[2,4,128,128]{3,2,1,0:T(8,128)} %param.12) | copy-start | bytes 1572868
  0.6 20.1 %copy-start.15 = (f32[4,256,256]{2,1,0:T(8,128)S(1)}, f32[4,256,256]{2,1,0:T(8,128)}, u32[]{:S(2)}) copy-start(f32[4,256,256]{2,1,0:T(8,128)} %param.11) | copy-start | bytes 3145732
  13.5 15.8 %all-to-all-start = ((s32[8,1,9]{2,1,0:T(1,128)}), s32[8,1,9]{2,1,0:T(1,128)S(1)}, u32[]{:S(2)}, u32[]{:S(2)}) async-start(s32[8,1,9]{2,1,0:T(1,128)} %bitcast.4), calls=%async_computation | async-start | bytes 8192 | tf_op jit(solution)/shard_map/all_to_all | solution.py:96
  21.1 4.3 copy-start.9
  26.5 3.2 collective-permute-start
  27.9 5.3 collective-permute-start.1
  33.4 5.4 collective-permute-start.2
  37.3 5.7 collective-permute-start.3
  56.5 57.4 %all-to-all-start.1 = ((f32[8,9,64,128]{3,2,1,0:T(8,128)}), f32[8,9,64,128]{3,2,1,0:T(8,128)}, u32[]{:S(2)}, u32[]{:S(2)}) async-start(f32[8,9,64,128]{3,2,1,0:T(8,128)} %broadcast_select_fusion.7), calls=%async_computation.1 | async-start | bytes 4718592 | tf_op jit(solution)/shard_map/all_to_all | solution.py:124
  131.4 62.8 %all-to-all-start.2 = ((f32[8,9,64,128]{3,2,1,0:T(8,128)}), f32[8,9,64,128]{3,2,1,0:T(8,128)}, u32[]{:S(2)}, u32[]{:S(2)}) async-start(f32[8,9,64,128]{3,2,1,0:T(8,128)} %broadcast_select_fusion.6), calls=%async_computation.2 | async-start | bytes 4718592 | tf_op jit(solution)/shard_map/all_to_all | solution.py:133
  204.2 6.3 copy-start.11
  204.2 3.6 collective-permute-start.4
  206.2 3.1 collective-permute-start.5
  212.0 7.7 collective-permute-start.7
  213.3 6.1 collective-permute-start.6
  219.5 5.1 copy-start.3
  220.8 3.8 copy-start.10
  319.0 2.8 collective-permute-start.8
  320.3 6.3 collective-permute-start.9
  326.7 4.7 collective-permute-start.10
  329.6 6.3 collective-permute-start.11
  495.3 3.3 collective-permute-start.12
  497.3 3.1 collective-permute-start.13
  504.0 5.1 collective-permute-start.14
  507.6 5.7 collective-permute-start.15
  514.4 3.8 copy-start.4
  611.2 17.4 %copy-start.1 = (f32[4,256,256]{1,2,0:T(8,128)}, f32[4,256,256]{1,2,0:T(8,128)S(1)}, u32[]{:S(2)}) copy-start(f32[4,256,256]{1,2,0:T(8,128)S(1)} %multiply_add_fusion.2) | copy-start | bytes 3145732
  611.4 2.8 collective-permute-start.16
  612.7 6.3 collective-permute-start.17
  619.1 5.3 collective-permute-start.18
  622.9 5.7 collective-permute-start.19
  787.2 3.3 collective-permute-start.20
  789.3 3.1 collective-permute-start.21
  796.0 5.1 collective-permute-start.22
  799.6 5.7 collective-permute-start.23
  806.4 3.9 copy-start.2
  806.4 3.9 copy-start.5
  903.5 17.3 %copy-start.7 = (f32[4,256,256]{1,2,0:T(8,128)}, f32[4,256,256]{1,2,0:T(8,128)S(1)}, u32[]{:S(2)}) copy-start(f32[4,256,256]{1,2,0:T(8,128)S(1)} %multiply_add_fusion.1) | copy-start | bytes 3145732
  903.7 2.8 collective-permute-start.24
  905.0 6.3 collective-permute-start.25
  911.4 5.2 collective-permute-start.26
  915.1 5.7 collective-permute-start.27
  1079.5 3.3 collective-permute-start.28
  1081.6 3.1 collective-permute-start.29
  1088.3 5.2 collective-permute-start.30
  1091.9 5.7 collective-permute-start.31
  1098.7 3.9 copy-start.6
  1098.7 3.9 copy-start.8
  (3 other events, 7.4 us)
where the time goes:
time: 1170 us; the launch traced here: 1150 us
  blocking collectives  632 us (54%)
  waiting for transfers between devices  157 us (13%)
  local copies, waits for them, and re-layouts  131 us (11%)
  matrix products  94.2 us (8%)
  starting transfers between devices  84.8 us (7%)
  other arithmetic  44.8 us (4%)
    psum x7, blocking collectives, global_sum(): return lax.psum(local_value, ('gx', 'gy'))  283 us
    all_to_all x3, blocking collectives, shards(): lax.all_to_all(returning, 'gy', split_axis=0, concat_axis=0, tiled=True)  180 us
    all_to_all x3, blocking collectives, shards(): lax.all_to_all(outgoing, 'gy', split_axis=0, concat_axis=0, tiled=True)  170 us
    all_to_all x1, waiting for transfers between devices, shards(): lax.all_to_all(returning, 'gy', split_axis=0, concat_axis=0, tiled=True)  54.4 us
    ppermute x16, waiting for transfers between devices, extended(): lax.ppermute(lax.slice_in_dim(block, 0, width, axis=dim), axis, backward)  53.8 us
    all_to_all x1, waiting for transfers between devices, shards(): lax.all_to_all(outgoing, 'gy', split_axis=0, concat_axis=0, tiled=True)  48.2 us
    ppermute x16, starting transfers between devices, extended(): lax.ppermute(lax.slice_in_dim(block, block.shape[dim] - width, None, axis...  42.3 us
  transfers between devices with their start and end apart: 35, of which 22 were waited for; matrix products, arithmetic and copies ran while one was open for 1% of the time, Pallas kernels for 0%

commit v1 on v0

--- a/solution.py
+++ b/solution.py
@@ -107,7 +107,13 @@
     precond_res = jacobi_inverse * residual
 
     def global_sum(local_value):
-        return lax.psum(local_value, ("gx", "gy"))
+
+        def attach_the_cube(vals):
+            for ii in ("gy", "gx"):
+                vals = lax.psum(vals, ii)
+            return vals
+
+        return attach_the_cube(local_value)
 
     direction = precond_res
     rho_now = global_sum(jnp.sum(residual * precond_res))

time: 1170 us -> 1060 us (0.906)
  blocking collectives: 632 us -> 526 us
    psum x7 -> x14, blocking collectives: 283 us -> 178 us  [attach_the_cube(): vals = lax.psum(vals, ii)]
where the time goes in v1:
time: 1060 us; the launch traced here: 1050 us
  blocking collectives  526 us (50%)
  waiting for transfers between devices  154 us (15%)
  local copies, waits for them, and re-layouts  131 us (12%)
  matrix products  94.2 us (9%)
  starting transfers between devices  88 us (8%)
  other arithmetic  44.8 us (4%)
  between operations  10.8 us (1%)
    all_to_all x3, blocking collectives, shards(): lax.all_to_all(returning, 'gy', split_axis=0, concat_axis=0, tiled=True)  179 us
    psum x14, blocking collectives, attach_the_cube(): vals = lax.psum(vals, ii)  178 us
    all_to_all x3, blocking collectives, shards(): lax.all_to_all(outgoing, 'gy', split_axis=0, concat_axis=0, tiled=True)  168 us
    all_to_all x1, waiting for transfers between devices, shards(): lax.all_to_all(returning, 'gy', split_axis=0, concat_axis=0, tiled=True)  54.3 us
    ppermute x16, waiting for transfers between devices, extended(): lax.ppermute(lax.slice_in_dim(block, 0, width, axis=dim), axis, backward)  50.4 us
    all_to_all x1, waiting for transfers between devices, shards(): lax.all_to_all(outgoing, 'gy', split_axis=0, concat_axis=0, tiled=True)  48.2 us
    ppermute x16, starting transfers between devices, extended(): lax.ppermute(lax.slice_in_dim(block, block.shape[dim] - width, None, axis...  45.6 us
    ppermute x16, starting transfers between devices, extended(): lax.ppermute(lax.slice_in_dim(block, 0, width, axis=dim), axis, backward)  22.2 us
  transfers between devices with their start and end apart: 35, of which 22 were waited for; matrix products, arithmetic and copies ran while one was open for 1% of the time, Pallas kernels for 0%

profile of v1, /device:TPU:0, one launch (start us, length us, event | category | flops | bytes accessed | tf_op | source)
XLA Modules:
  0.0 1047.8 jit_solution(9646645353159933572)
XLA Ops:
  3.4 10.2 scatter_fusion
  13.6 7.3 all-to-all-start
  33.5 3.9 collective-permute-start.2
  38.9 4.2 collective-permute-done.3
  56.6 5.8 all-to-all-start.1
  66.0 48.2 %all-to-all-done.1 = f32[8,9,64,128]{3,2,1,0:T(8,128)} async-done(((f32[8,9,64,128]{3,2,1,0:T(8,128)}), f32[8,9,64,128]{3,2,1,0:T(8,128)}, u32[]{:S(2)}, u32[]{:S(2)}) %all-to-all-start.1) | async-done | bytes 2359328 | tf_op jit(solution)/shard_map/all_to_all | solution.py:130
  131.5 7.1 all-to-all-start.2
  140.0 54.3 %all-to-all-done.2 = f32[8,9,64,128]{3,2,1,0:T(8,128)} async-done(((f32[8,9,64,128]{3,2,1,0:T(8,128)}), f32[8,9,64,128]{3,2,1,0:T(8,128)}, u32[]{:S(2)}, u32[]{:S(2)}) %all-to-all-start.2) | async-done | bytes 2359328 | tf_op jit(solution)/shard_map/all_to_all | solution.py:139
  213.4 4.5 collective-permute-start.6
  220.9 3.8 fusion.18
  224.7 4.5 multiply_reduce_fusion.6
  229.3 21.4 %all-reduce = (f32[]{:T(128)}, f32[]{:T(128)}) all-reduce(f32[]{:T(128)} %get-tuple-element.7, f32[]{:T(128)} %get-tuple-element.6), channel_id=1, replica_groups=mesh['gx'=4,'gy'=8] {'gy'}, use_global_device_ids=true, to_apply=%region_1.2 | all-reduce | flops 2 | bytes 16 | tf_op jit(solution)/shard_map/psum | solution.py:113
  250.7 6.3 all-reduce.1
  258.4 4.0 multiply_reduce_fusion.5
  262.4 17.8 %psum.116 = f32[]{:T(128)} all-reduce(f32[]{:T(128)} %get-tuple-element.18), channel_id=1, replica_groups=mesh['gx'=4,'gy'=8] {'gy'}, use_global_device_ids=true, to_apply=%region_11.14 | all-reduce | flops 1 | bytes 8 | tf_op jit(solution)/shard_map/psum | solution.py:113
  280.1 6.3 psum.117
  296.8 3.9 collective-permute-start.10
  302.2 4.2 collective-permute-done.11
  322.9 56.1 %all_to_all.52 = f32[8,9,64,128]{3,2,1,0:T(8,128)} all-to-all(f32[8,9,64,128]{3,2,1,0:T(8,128)S(1)} %broadcast_select_fusion.5), channel_id=1, replica_groups=mesh['gx'=4,'gy'=8] {'gy'}, dimensions={0} | all-to-all | bytes 4718592 | tf_op jit(solution)/shard_map/all_to_all | solution.py:130
  394.9 59.8 %all_to_all.53 = f32[8,9,64,128]{3,2,1,0:T(8,128)S(1)} all-to-all(f32[8,9,64,128]{3,2,1,0:T(8,128)S(1)} %broadcast_select_fusion.4), channel_id=1, replica_groups=mesh['gx'=4,'gy'=8] {'gy'}, dimensions={0} | all-to-all | bytes 4718592 | tf_op jit(solution)/shard_map/all_to_all | solution.py:139
  478.6 4.2 collective-permute-done.15
  483.8 3.8 fusion.38
  487.7 4.5 multiply_reduce_fusion.4
  492.2 19.4 %psum.118 = f32[]{:T(128)} all-reduce(f32[]{:T(128)} %get-tuple-element.59), channel_id=1, replica_groups=mesh['gx'=4,'gy'=8] {'gy'}, use_global_device_ids=true, to_apply=%region_14.17 | all-reduce | flops 1 | bytes 8 | tf_op jit(solution)/shard_map/psum | solution.py:113
  511.6 6.3 psum.119
  519.2 4.0 multiply_reduce_fusion.3
  523.2 18.1 %psum.120 = f32[]{:T(128)} all-reduce(f32[]{:T(128)} %get-tuple-element.15), channel_id=1, replica_groups=mesh['gx'=4,'gy'=8] {'gy'}, use_global_device_ids=true, to_apply=%region_17.20 | all-reduce | flops 1 | bytes 8 | tf_op jit(solution)/shard_map/psum | solution.py:113
  541.3 6.3 psum.121
  563.4 3.9 collective-permute-done.19
  583.8 56.1 %all_to_all.54 = f32[8,9,64,128]{3,2,1,0:T(8,128)} all-to-all(f32[8,9,64,128]{3,2,1,0:T(8,128)S(1)} %broadcast_select_fusion.3), channel_id=1, replica_groups=mesh['gx'=4,'gy'=8] {'gy'}, dimensions={0} | all-to-all | bytes 4718592 | tf_op jit(solution)/shard_map/all_to_all | solution.py:130
  655.8 59.7 %all_to_all.55 = f32[8,9,64,128]{3,2,1,0:T(8,128)S(1)} all-to-all(f32[8,9,64,128]{3,2,1,0:T(8,128)S(1)} %broadcast_select_fusion.2), channel_id=1, replica_groups=mesh['gx'=4,'gy'=8] {'gy'}, dimensions={0} | all-to-all | bytes 4718592 | tf_op jit(solution)/shard_map/all_to_all | solution.py:139
  739.5 4.2 collective-permute-done.23
  744.7 3.9 fusion.58
  748.7 4.5 multiply_reduce_fusion.2
  753.2 19.4 %psum.122 = f32[]{:T(128)} all-reduce(f32[]{:T(128)} %get-tuple-element.61), channel_id=1, replica_groups=mesh['gx'=4,'gy'=8] {'gy'}, use_global_device_ids=true, to_apply=%region_20.23 | all-reduce | flops 1 | bytes 8 | tf_op jit(solution)/shard_map/psum | solution.py:113
  772.6 6.3 psum.123
  780.1 4.1 multiply_reduce_fusion.1
  784.2 18.2 %psum.124 = f32[]{:T(128)} all-reduce(f32[]{:T(128)} %get-tuple-element.12), channel_id=1, replica_groups=mesh['gx'=4,'gy'=8] {'gy'}, use_global_device_ids=true, to_apply=%region_23.26 | all-reduce | flops 1 | bytes 8 | tf_op jit(solution)/shard_map/psum | solution.py:113
  802.3 6.3 psum.125
  824.5 4.2 collective-permute-done.27
  831.1 3.8 fusion.193
  845.2 56.1 %all_to_all.56 = f32[8,9,64,128]{3,2,1,0:T(8,128)} all-to-all(f32[8,9,64,128]{3,2,1,0:T(8,128)S(1)} %broadcast_select_fusion.1), channel_id=1, replica_groups=mesh['gx'=4,'gy'=8] {'gy'}, dimensions={0} | all-to-all | bytes 4718592 | tf_op jit(solution)/shard_map/all_to_all | solution.py:130
  917.2 59.9 %all_to_all.57 = f32[8,9,64,128]{3,2,1,0:T(8,128)S(1)} all-to-all(f32[8,9,64,128]{3,2,1,0:T(8,128)S(1)} %broadcast_select_fusion), channel_id=1, replica_groups=mesh['gx'=4,'gy'=8] {'gy'}, dimensions={0} | all-to-all | bytes 4718592 | tf_op jit(solution)/shard_map/all_to_all | solution.py:139
  1001.4 4.0 collective-permute-done.31
  1006.5 3.9 fusion.78
  1010.4 4.5 multiply_reduce_fusion
  1014.9 19.4 %psum.126 = f32[]{:T(128)} all-reduce(f32[]{:T(128)} %get-tuple-element.63), channel_id=1, replica_groups=mesh['gx'=4,'gy'=8] {'gy'}, use_global_device_ids=true, to_apply=%region_26.29 | all-reduce | flops 1 | bytes 8 | tf_op jit(solution)/shard_map/psum | solution.py:113
  1034.3 6.3 psum.127
  (232 shorter events, 287.9 us)
Async XLA Ops:
  0.6 117.2 %copy-start = (f32[2,4,128,128]{3,2,1,0:T(8,128)S(1)}, f32[2,4,128,128]{3,2,1,0:T(8,128)}, u32[]{:S(2)}) copy-start(f32[2,4,128,128]{3,2,1,0:T(8,128)} %param.12) | copy-start | bytes 1572868
  0.6 20.2 %copy-start.15 = (f32[4,256,256]{2,1,0:T(8,128)S(1)}, f32[4,256,256]{2,1,0:T(8,128)}, u32[]{:S(2)}) copy-start(f32[4,256,256]{2,1,0:T(8,128)} %param.11) | copy-start | bytes 3145732
  13.6 15.8 %all-to-all-start = ((s32[8,1,9]{2,1,0:T(1,128)}), s32[8,1,9]{2,1,0:T(1,128)S(1)}, u32[]{:S(2)}, u32[]{:S(2)}) async-start(s32[8,1,9]{2,1,0:T(1,128)} %bitcast.4), calls=%async_computation | async-start | bytes 8192 | tf_op jit(solution)/shard_map/all_to_all | solution.py:96
  21.2 4.3 copy-start.9
  26.6 3.2 collective-permute-start
  28.1 5.3 collective-permute-start.1
  33.5 5.4 collective-permute-start.2
  37.4 5.7 collective-permute-start.3
  56.6 57.6 %all-to-all-start.1 = ((f32[8,9,64,128]{3,2,1,0:T(8,128)}), f32[8,9,64,128]{3,2,1,0:T(8,128)}, u32[]{:S(2)}, u32[]{:S(2)}) async-start(f32[8,9,64,128]{3,2,1,0:T(8,128)} %broadcast_select_fusion.7), calls=%async_computation.1 | async-start | bytes 4718592 | tf_op jit(solution)/shard_map/all_to_all | solution.py:130
  131.5 62.8 %all-to-all-start.2 = ((f32[8,9,64,128]{3,2,1,0:T(8,128)}), f32[8,9,64,128]{3,2,1,0:T(8,128)}, u32[]{:S(2)}, u32[]{:S(2)}) async-start(f32[8,9,64,128]{3,2,1,0:T(8,128)} %broadcast_select_fusion.6), calls=%async_computation.2 | async-start | bytes 4718592 | tf_op jit(solution)/shard_map/all_to_all | solution.py:139
  204.3 6.3 copy-start.11
  204.3 3.9 collective-permute-start.4
  206.3 3.1 collective-permute-start.5
  212.1 7.7 collective-permute-start.7
  213.4 6.1 collective-permute-start.6
  219.6 5.1 copy-start.3
  220.9 3.8 copy-start.10
  289.2 3.7 collective-permute-start.8
  291.4 5.3 collective-permute-start.9
  296.8 5.4 collective-permute-start.10
  300.7 5.7 collective-permute-start.11
  464.7 3.3 collective-permute-start.12
  466.7 3.1 collective-permute-start.13
  473.5 4.9 collective-permute-start.14
  477.1 5.7 collective-permute-start.15
  483.8 3.8 copy-start.4
  550.3 17.1 %copy-start.1 = (f32[4,256,256]{1,2,0:T(8,128)}, f32[4,256,256]{1,2,0:T(8,128)S(1)}, u32[]{:S(2)}) copy-start(f32[4,256,256]{1,2,0:T(8,128)S(1)} %multiply_add_fusion.2) | copy-start | bytes 3145732
  550.5 3.7 collective-permute-start.16
  552.7 5.3 collective-permute-start.17
  558.1 5.3 collective-permute-start.18
  561.6 5.7 collective-permute-start.19
  725.6 3.3 collective-permute-start.20
  727.6 3.1 collective-permute-start.21
  734.4 4.9 collective-permute-start.22
  738.0 5.7 collective-permute-start.23
  744.7 3.9 copy-start.2
  744.7 3.9 copy-start.5
  811.7 17.1 %copy-start.7 = (f32[4,256,256]{1,2,0:T(8,128)}, f32[4,256,256]{1,2,0:T(8,128)S(1)}, u32[]{:S(2)}) copy-start(f32[4,256,256]{1,2,0:T(8,128)S(1)} %multiply_add_fusion.1) | copy-start | bytes 3145732
  811.9 3.7 collective-permute-start.24
  814.1 5.3 collective-permute-start.25
  819.4 5.1 collective-permute-start.26
  823.0 5.7 collective-permute-start.27
  987.3 3.3 collective-permute-start.28
  989.3 3.1 collective-permute-start.29
  996.1 5.1 collective-permute-start.30
  999.7 5.7 collective-permute-start.31
  1006.5 3.9 copy-start.6
  1006.5 3.9 copy-start.8
  (3 other events, 7.4 us)
